TPU v7x, 32 devices: a whole 2x2x4 slice. The times are simulated.
32 devices in a mesh: grp: 4 (over x, core), tp: 8 (over z, y).
Axes of the slice: x: 2, y: 2, z: 4, core: 2. Of those that a mesh axis runs over, the one named last changes fastest.
Arguments:
- hidden_in: bfloat16 [3072, 3584], P('grp'), may hold values from -6 to 6
- lengths: int32 [8, 8], P('grp'), may hold values from 1 to 96, 384 in all within a row
- dest: int32 [64, 1], P('grp'), may hold values from 0 to 3; in each aligned block of 16 rows (0 to 15, 16 to 31, ...) at most 4 rows name the same one
- attn_gain: float32 [3584], replicated, may hold values from 0.6 to 8
- q_weight: bfloat16 [3584, 2048], P('grp', 'tp'), may hold values from -0.09375 to 0.09375
- k_weight: bfloat16 [3584, 512], P('grp', 'tp'), may hold values from -0.09375 to 0.09375
- v_weight: bfloat16 [3584, 512], P('grp', 'tp'), may hold values from -0.09375 to 0.09375
- o_weight: bfloat16 [3584, 2048], P('grp', 'tp'), may hold values from -0.125 to 0.125
- ffn_gain: float32 [3584], replicated, may hold values from 0.1 to 1.9
- gate_weight: bfloat16 [3584, 10240], P('grp', 'tp'), may hold values from -0.09375 to 0.09375
- up_weight: bfloat16 [3584, 10240], P('grp', 'tp'), may hold values from -0.09375 to 0.09375
- down_weight: bfloat16 [3584, 10240], P('grp', 'tp'), may hold values from -0.0625 to 0.0625
Outputs:
- bank_in: bfloat16 [4, 4, 4, 3584], P('grp', None, None, 'tp')
Inputs may be any that keep to these rules, and one draw needn't show every extreme that they name: Each block's 8 lengths sum to 384. `dest`: among the programs of one index of grp, no bank shard is named by more than 4.
All inputs are finite; a program needn't handle non-finite values.
Results may differ from a plain program's by a relative error of at most 0.015.
The roundings to bfloat16 on the way count: a program that leaves them out, or rounds other values in their place, can miss the bound.
Values may be sent and summed in bfloat16 or wider, within the bound.
No kernel may reach another device: no remote copies, remote signals or barrier semaphores. Data moves between devices by JAX's collectives and lax.ppermute only.
A program may use at most 128 MiB of HBM per device.

v0:
```python
import jax
import jax.numpy as jnp
from jax import lax
from jax.sharding import PartitionSpec as P

HEAD_SIZE = 128
KVH = 4
HEADS = 16
EPSILON = 1e-06
HIGH = lax.Precision.HIGHEST


def rms_scale(rows, gain):
    rows = rows.astype(jnp.float32)
    factor = lax.rsqrt(jnp.mean(rows * rows, axis=1, keepdims=True) + EPSILON)
    return (rows * factor * gain[None, :]).astype(jnp.bfloat16)


def segment_ids(lengths, block_rows):
    bounds = jnp.cumsum(lengths, axis=1)
    position = lax.broadcasted_iota(jnp.int32, (lengths.shape[0], block_rows), 1)
    return jnp.sum((position[:, :, None] >= bounds[:, None, :]).astype(jnp.int32), axis=2)


def softmax_rows(attention_scores):
    top = jnp.max(attention_scores, axis=-1, keepdims=True)
    expo = jnp.exp(attention_scores - top)
    return (expo / jnp.sum(expo, axis=-1, keepdims=True)).astype(jnp.bfloat16)


def transposed_dot(left, right):
    return lax.dot_general(
        left, right, (((1,), (1,)), ((), ())), preferred_element_type=jnp.float32
    )


def gather_grp(piece, chips):
    held = [piece]
    moving = piece
    if chips > 1:
        ring = [(2 * i + c, 2 * ((i + 1) % chips) + c) for i in range(chips) for c in range(2)]
        for _ in range(chips - 1):
            moving = lax.ppermute(moving, "grp", ring)
            held.append(moving)
    mine = jnp.stack(held)
    other = lax.ppermute(mine, "grp", [(g, g ^ 1) for g in range(2 * chips)])
    return jnp.concatenate([mine, other], 0)


def source_order(chips):
    g = lax.axis_index("grp")
    chip, core = (g // 2, g % 2)
    steps = jnp.arange(chips, dtype=jnp.int32)
    own = 2 * ((chip - steps) % chips) + core
    return jnp.concatenate([own, own - core + (1 - core)])


def take_blocks(x, order, size, axis):
    return jnp.concatenate(
        [lax.dynamic_slice_in_dim(x, order[k] * size, size, axis) for k in range(order.shape[0])],
        axis,
    )


def on_device(
    hidden_in,
    lengths,
    dest,
    attn_gain,
    q_weight,
    k_weight,
    v_weight,
    o_weight,
    ffn_gain,
    gate_weight,
    up_weight,
    down_weight,
):
    row_count, width = hidden_in.shape
    blocks, per_block = lengths.shape
    block_rows = row_count // blocks
    programs = blocks * per_block
    tp_size = lax.axis_size("tp")
    grp_size = lax.axis_size("grp")
    chips = grp_size // 2
    tp_index = lax.axis_index("tp")
    grp_index = lax.axis_index("grp")
    d_grp = width // grp_size
    d_tp = width // tp_size
    ratio = tp_size // grp_size
    capacity = max(2, (programs + grp_size - 1) // grp_size)
    local_heads = q_weight.shape[1] // HEAD_SIZE
    order = source_order(chips)
    q_cols, k_cols = (q_weight.shape[1], k_weight.shape[1])
    qkv_full = gather_grp(jnp.concatenate([q_weight, k_weight, v_weight], 1), chips)
    qkv_full = qkv_full.reshape(width, -1)
    o_full = gather_grp(o_weight, chips).reshape(width, -1)
    gate_full = gather_grp(gate_weight, chips).reshape(width, -1)
    up_full = gather_grp(up_weight, chips).reshape(width, -1)
    hidden_perm = take_blocks(hidden_in, order, d_grp, 1)
    attn_gain_perm = take_blocks(attn_gain, order, d_grp, 0)
    ffn_gain_perm = take_blocks(ffn_gain, order, d_grp, 0)
    norm_in = rms_scale(hidden_perm, attn_gain_perm)
    qkv = jnp.dot(norm_in, qkv_full, preferred_element_type=jnp.float32).astype(jnp.bfloat16)
    queries = qkv[:, :q_cols]
    kv_part = qkv[:, q_cols:]
    kv_all = lax.all_to_all(
        jnp.broadcast_to(kv_part[None], (tp_size,) + kv_part.shape), "tp", 0, 0, tiled=True
    )
    per_dev = k_cols // KVH
    kv_index = tp_index * local_heads // (HEADS // KVH)

    def head_of(part):
        split = part.reshape(tp_size, row_count, per_dev, KVH)
        one = lax.dynamic_slice_in_dim(split, kv_index, 1, 3)[..., 0]
        return one.transpose(1, 0, 2).reshape(row_count, tp_size * per_dev)

    key_head = head_of(kv_all[:, :, :k_cols])
    value_head = head_of(kv_all[:, :, k_cols:])
    segs = segment_ids(lengths, block_rows)
    same = segs[:, :, None] == segs[:, None, :]
    blocked_queries = queries.reshape(blocks, block_rows, local_heads, HEAD_SIZE)
    blocked_keys = key_head.reshape(blocks, block_rows, HEAD_SIZE)
    blocked_values = value_head.reshape(blocks, block_rows, HEAD_SIZE)
    attention_scores = jnp.einsum(
        "xwre,xpe->xrwp", blocked_queries, blocked_keys, preferred_element_type=jnp.float32
    ) * HEAD_SIZE ** (-0.5)
    attention_scores = jnp.where(same[:, None, :, :], attention_scores, -1e30)
    attention_probabilities = softmax_rows(attention_scores)
    attended_rows = jnp.einsum(
        "asfo,aon->afsn",
        attention_probabilities,
        blocked_values,
        preferred_element_type=jnp.float32,
    )
    attended_rows = attended_rows.astype(jnp.bfloat16).reshape(row_count, local_heads * HEAD_SIZE)
    attn_term = transposed_dot(attended_rows, o_full)
    attn_total = lax.psum(attn_term.astype(jnp.bfloat16), "tp").astype(jnp.float32)
    residual = hidden_perm.astype(jnp.float32) + attn_total
    norm_mid = rms_scale(residual, ffn_gain_perm)
    gate_pre = jnp.dot(norm_mid, gate_full, preferred_element_type=jnp.float32)
    up_pre = jnp.dot(norm_mid, up_full, preferred_element_type=jnp.float32)
    hidden_ffn = (jax.nn.silu(gate_pre) * up_pre).astype(jnp.bfloat16)
    block_index = lax.broadcasted_iota(jnp.int32, (blocks, block_rows), 0)
    program_of_row = (block_index * per_block + segs).reshape(row_count)
    program_grid = lax.broadcasted_iota(jnp.int32, (programs, row_count), 0)
    selector = (program_grid == program_of_row[None, :]).astype(jnp.float32)
    hidden_sums = jnp.dot(
        selector.astype(jnp.bfloat16), hidden_ffn, preferred_element_type=jnp.float32
    )
    chunk_owner = tp_index // ratio
    owner_step = jnp.argmax(order == chunk_owner).astype(jnp.int32)
    chunk_start = owner_step * d_grp + tp_index % ratio * d_tp
    residual_chunk = lax.dynamic_slice_in_dim(residual, chunk_start, d_tp, 1)
    residual_sums = jnp.dot(
        selector, residual_chunk, precision=HIGH, preferred_element_type=jnp.float32
    )
    hidden_all = gather_grp(hidden_sums, chips).reshape(grp_size * programs, -1)
    down_part = lax.dot_general(
        hidden_all,
        down_weight.astype(jnp.float32),
        (((1,), (1,)), ((), ())),
        precision=HIGH,
        preferred_element_type=jnp.float32,
    )
    dest_all = gather_grp(dest[:, 0], chips)
    lengths_all = gather_grp(lengths.reshape(programs), chips).reshape(grp_size * programs)
    grp_ids = lax.broadcasted_iota(jnp.int32, (grp_size, programs, grp_size), 2)
    chosen = (dest_all[:, :, None] == grp_ids).astype(jnp.int32)
    earlier = jnp.cumsum(chosen, axis=1) - chosen
    slot_rank = jnp.sum(earlier * chosen, axis=2)
    slot_row = order[:, None] * capacity + slot_rank
    slots = grp_size * capacity
    target_grid = lax.broadcasted_iota(jnp.int32, (grp_size, slots, grp_size, programs), 0)
    row_grid = lax.broadcasted_iota(jnp.int32, (grp_size, slots, grp_size, programs), 1)
    placer = (
        ((target_grid == dest_all[None, None]) & (row_grid == slot_row[None, None]))
        .astype(jnp.float32)
        .reshape(grp_size, slots, grp_size * programs)
    )
    down_slots = jnp.einsum("asq,qd->asd", placer, down_part, precision=HIGH)
    down_slots = down_slots.reshape(grp_size, slots, ratio, d_tp).transpose(0, 2, 1, 3)
    send = lax.dynamic_update_slice(
        jnp.zeros((grp_size, tp_size, slots, d_tp), jnp.float32),
        down_slots,
        (0, grp_index * ratio, 0, 0),
    )
    local_placer = placer[:, :, :programs]
    residual_slots = jnp.einsum("asq,qd->asd", local_placer, residual_sums, precision=HIGH)
    send = send + lax.dynamic_update_slice(
        jnp.zeros((grp_size, tp_size, slots, d_tp), jnp.float32),
        residual_slots[:, None],
        (0, tp_index, 0, 0),
    )
    received = lax.all_to_all(
        send.reshape(grp_size * tp_size, slots, d_tp), ("grp", "tp"), 0, 0, tiled=True
    )
    totals = jnp.sum(received, axis=0)
    mine = lax.dynamic_index_in_dim(placer, grp_index, 0, keepdims=False)
    counts = jnp.dot(mine, lengths_all.astype(jnp.float32), precision=HIGH)
    counts = jnp.where(counts > 0, counts, 1.0)
    embedded = (totals / counts[:, None]).astype(jnp.bfloat16)
    return embedded.reshape(1, grp_size, capacity, d_tp)


def solution(mesh):
    placed = (
        P("grp", None),
        P("grp", None),
        P("grp", None),
        P(),
        P("grp", "tp"),
        P("grp", "tp"),
        P("grp", "tp"),
        P("grp", "tp"),
        P(),
        P("grp", "tp"),
        P("grp", "tp"),
        P("grp", "tp"),
    )
    return jax.shard_map(
        on_device, mesh=mesh, in_specs=placed, out_specs=P("grp", None, None, "tp"), check_vma=False
    )
```

profile of v0, /device:TPU:0, one launch (start us, length us, event | category | flops | bytes accessed | tf_op | source)
XLA Modules:
  0.0 450.6 jit_solution(4661509185440796981)
XLA Ops:
  6.5 1.2 copy.59
  7.8 1.1 copy.60
  8.8 2.0 pad_maximum_fusion.9
  10.9 2.9 collective-permute-start.2
  15.7 1.2 fusion.76
  16.9 13.5 %collective-permute-done.2 = bf16[896,384]{1,0:T(8,128)(2,1)} collective-permute-done((bf16[896,384]{1,0:T(8,128)(2,1)}, bf16[896,384]{1,0:T(8,128)(2,1)}, u32[]{:S(2)}, u32[]{:S(2)}) %collective-permute-start.2) | collective-permute-done | bytes 688160 | tf_op jit(solution)/shard_map/ppermute | solution.py:43
  30.4 2.4 pad_maximum_fusion.7
  32.7 0.6 fusion.62
  34.7 3.1 constant_dynamic-slice_fusion.5
  37.8 1.4 fusion.1
  39.2 2.3 pad_maximum_fusion.5
  41.5 4.1 fusion.12
  45.6 0.8 copy-done.13
  46.6 1.2 broadcast_in_dim.19
  47.8 6.4 %all-to-all-start = ((bf16[8,768,128]{1,2,0:T(8,128)(2,1)}), bf16[8,768,128]{1,2,0:T(8,128)(2,1)}, u32[]{:S(2)}, u32[]{:S(2)}) async-start(bf16[8,768,128]{1,2,0:T(8,128)(2,1)} %broadcast_in_dim.19), calls=%async_computation | async-start | bytes 3145728 | tf_op jit(solution)/shard_map/all_to_all | solution.py:107
  54.3 1.5 collective-permute-start.8
  56.4 81.2 %collective-permute-done.4 = bf16[896,256]{1,0:T(8,128)(2,1)S(1)} collective-permute-done((bf16[896,256]{1,0:T(8,128)(2,1)S(1)}, bf16[896,256]{1,0:T(8,128)(2,1)S(1)}, u32[]{:S(2)}, u32[]{:S(2)}) %collective-permute-start.4) | collective-permute-done | bytes 458784 | tf_op jit(solution)/shard_map/ppermute | solution.py:43
  137.6 1.0 pad_maximum_fusion.8
  138.9 0.9 broadcast_compare_fusion
  139.8 1.6 collective-permute-done.5
  141.4 2.6 pad_maximum_fusion.6
  144.0 1.0 slice.47
  145.0 0.9 reshape.188
  145.9 5.1 %pad_maximum_fusion.3 = bf16[2,896,1280]{2,1,0:T(8,128)(2,1)} fusion(bf16[1,896,1280]{2,1,0:T(8,128)(2,1)} %bitcast.25, bf16[1,896,1280]{2,1,0:T(8,128)(2,1)} %bitcast.96), kind=kLoop, calls=%fused_computation.16 | loop fusion | flops 2293760 | bytes 9175040 | tf_op jit(solution)/shard_map/stack | solution.py:45
  151.1 4.1 pad_maximum_fusion.4
  155.6 1.5 fusion.58
  158.3 3.5 fusion.63
  161.8 2.0 fusion.15
  164.4 5.6 %convolution_convert_fusion = bf16[768,3584]{1,0:T(8,128)(2,1)} fusion(bf16[3584,256]{1,0:T(8,128)(2,1)} %bitcast.102, bf16[96,8,2,128]{3,2,1,0:T(2,128)(2,1)S(1)} %bitcast.105), kind=kOutput, calls=%fused_computation.11 | convolution fusion | flops 1412038656 | bytes 7733248 | tf_op jit(solution)/shard_map/dot_general | solution.py:32
  170.1 1.7 collective-permute-start.12
  172.5 0.8 compare_reduce_fusion
  174.4 1.0 collective-permute-done
  175.5 1.1 collective-permute-done.1
  177.0 9.9 %pad_maximum_fusion = bf16[4,896,1280]{2,1,0:T(8,128)(2,1)} fusion(bf16[2,896,1280]{2,1,0:T(8,128)(2,1)} %collective-permute-done.7, bf16[1,896,1280]{2,1,0:T(8,128)(2,1)} %bitcast.25, bf16[1,896,1280]{2,1,0:T(8,128)(2,1)} %bitcast.97), kind=kLoop, calls=%fused_computation.9 | loop fusion | flops 9175040 | bytes 18350080 | tf_op jit(solution)/shard_map/concatenate | solution.py:47
  186.9 8.2 %pad_maximum_fusion.1 = bf16[4,896,1280]{2,1,0:T(8,128)(2,1)} fusion(bf16[2,896,1280]{2,1,0:T(8,128)(2,1)} %collective-permute-done.9, bf16[1,896,1280]{2,1,0:T(8,128)(2,1)} %bitcast.28, bf16[1,896,1280]{2,1,0:T(8,128)(2,1)S(1)} %bitcast.99), kind=kLoop, calls=%fused_computation.10 | loop fusion | flops 9175040 | bytes 18350080 | tf_op jit(solution)/shard_map/concatenate | solution.py:47
  195.1 167.2 %all-reduce.2.cloned.1.call-done = bf16[768,3584]{1,0:T(8,128)(2,1)} async-done(((bf16[768,3584]{1,0:T(8,128)(2,1)}), bf16[768,3584]{1,0:T(8,128)(2,1)}) %all-reduce.2.cloned.1.call-update) | async-done | bytes 5505040 | tf_op jit(solution)/shard_map/psum | solution.py:138
  362.4 11.9 %convert_add_fusion = (f32[768,3584]{1,0:T(8,128)}, f32[768]{0:T(1024)S(1)}) fusion(bf16[768,3584]{1,0:T(8,128)(2,1)} %all-reduce.2.cloned.1.call-done, bf16[768,896]{1,0:T(8,128)(2,1)} %copy-done.5, bf16[768,896]{1,0:T(8,128)(2,1)} %copy-done.7, bf16[768,896]{1,0:T(8,128)(2,1)} %copy-done.3, bf16[768,896]{1,0:T(8,128)(2,1)} %copy-done.1), kind=kLoop, calls=%fused_computation.1 | loop fusion | flops 33029376 | bytes 22023168 | tf_op jit(solution)/shard_map/add | solution.py:139
  374.3 11.6 %fusion.56 = f32[768,1280]{1,0:T(8,128)} fusion(bf16[3584,1280]{1,0:T(8,128)(2,1)S(1)} %bitcast.101, f32[3584]{0:T(1024)S(1)} %pad_maximum_fusion.13, f32[768]{0:T(1024)S(1)} %add_rsqrt_fusion, bf16[768,3584]{1,0:T(8,128)(2,1)} %all-reduce.2.cloned.1.call-done, bf16[768,896]{1,0:T(8,128)(2,1)S(1)} %copy-done.6, bf16[768,896]{1,0:T(8,128)(2,1)S(1)} %copy-done.8, ...), kind=kOutput, calls=%fused_computation.111 | convolution fusion | flops 7082213376 | bytes 24134656 | tf_op jit(solution)/shard_map/dot_general | solution.py:142
  386.0 14.4 %fusion.9 = f32[16,1280]{1,0:T(8,128)S(1)} fusion(f32[768,1280]{1,0:T(8,128)} %fusion.56, s32[768]{0:T(1024)S(1)} %add.143, bf16[3584,1280]{1,0:T(8,128)(2,1)} %bitcast.100, f32[3584]{0:T(1024)S(1)} %pad_maximum_fusion.13, f32[768]{0:T(1024)S(1)} %add_rsqrt_fusion, bf16[768,3584]{1,0:T(8,128)(2,1)} %all-reduce.2.cloned.1.call-done, ...), kind=kOutput, calls=%fused_computation.24 | convolution fusion | flops 7119605760 | bytes 24219648 | tf_op jit(solution)/shard_map/dot_general | solution.py:148
  400.4 1.5 collective-permute-start.10
  402.2 2.8 collective-permute-done.10
  405.2 2.3 fusion.21
  407.6 2.1 convolution_bitcast_fusion.1
  410.6 1.1 copy.73
  411.7 3.7 all-to-all-start.1
  415.7 0.9 collective-permute-done.13
  416.9 26.1 %all-to-all-done.1 = f32[32,16,448]{2,1,0:T(8,128)S(1)} async-done(((f32[32,16,448]{2,1,0:T(8,128)}), f32[32,16,448]{2,1,0:T(8,128)S(1)}, u32[]{:S(2)}, u32[]{:S(2)}) %all-to-all-start.1) | async-done | bytes 917536 | tf_op jit(solution)/shard_map/all_to_all | solution.py:195
  443.1 0.7 divide_convert_fusion.2
  (109 shorter events, 7.8 us)
Async XLA Ops:
  6.5 401.0 %copy-start = (bf16[896,1280]{1,0:T(8,128)(2,1)S(1)}, bf16[896,1280]{1,0:T(8,128)(2,1)}, u32[]{:S(2)}) copy-start(bf16[896,1280]{1,0:T(8,128)(2,1)} %param.23) | copy-start | bytes 6881284
  6.5 28.0 %copy-start.14 = (f32[3584]{0:T(1024)S(1)}, f32[3584]{0:T(1024)}, u32[]{:S(2)}) copy-start(f32[3584]{0:T(1024)} %param.15) | copy-start | bytes 43012
  10.9 19.5 %collective-permute-start.2 = (bf16[896,384]{1,0:T(8,128)(2,1)}, bf16[896,384]{1,0:T(8,128)(2,1)}, u32[]{:S(2)}, u32[]{:S(2)}) collective-permute-start(bf16[896,384]{1,0:T(8,128)(2,1)} %pad_maximum_fusion.9), channel_id=1, source_target_pairs={{0,16},{8,24},{16,0},{24,8},{1,17},{9,25},{17,1},{25,9},{2,18},{10... | collective-permute-start | bytes 2064392 | tf_op jit(solution)/shard_map/ppermute | solution.py:43
  13.8 132.1 %collective-permute-start.6 = (bf16[896,1280]{1,0:T(8,128)(2,1)}, bf16[896,1280]{1,0:T(8,128)(2,1)}, u32[]{:S(2)}, u32[]{:S(2)}) collective-permute-start(bf16[896,1280]{1,0:T(8,128)(2,1)} %param.21), channel_id=1, source_target_pairs={{0,16},{8,24},{16,0},{24,8},{1,17},{9,25},{17,1},{25,9},{2,18},{10... | collective-permute-start | bytes 6881288 | tf_op jit(solution)/shard_map/ppermute | solution.py:43
  32.7 6.4 %collective-permute-start.3 = (bf16[2,896,384]{2,1,0:T(8,128)(2,1)}, bf16[2,896,384]{2,1,0:T(8,128)(2,1)}, u32[]{:S(2)}, u32[]{:S(2)}) collective-permute-start(bf16[2,896,384]{2,1,0:T(8,128)(2,1)} %pad_maximum_fusion.7), channel_id=1, source_target_pairs={{0,8},{8,0},{16,24},{24,16},{1,9},{9,1},{17,25},{25,17},{2,10},{10... | collective-permute-start | bytes 4128776 | tf_op jit(solution)/shard_map/ppermute | solution.py:46
  37.7 3.7 copy-start.1
  37.7 3.7 copy-start.3
  37.7 3.7 copy-start.5
  37.8 3.7 copy-start.7
  45.6 0.8 copy-start.13
  46.4 9.4 %copy-start.12 = (bf16[896,256]{1,0:T(8,128)(2,1)S(1)}, bf16[896,256]{1,0:T(8,128)(2,1)}, u32[]{:S(2)}) copy-start(bf16[896,256]{1,0:T(8,128)(2,1)} %param.19) | copy-start | bytes 1376260
  46.4 92.2 %copy-start.17 = (s32[2,8]{1,0:T(2,128)S(1)}, s32[2,8]{1,0:T(2,128)}, u32[]{:S(2)}) copy-start(s32[2,8]{1,0:T(2,128)} %param.13) | copy-start | bytes 196
  47.8 107.8 %all-to-all-start = ((bf16[8,768,128]{1,2,0:T(8,128)(2,1)}), bf16[8,768,128]{1,2,0:T(8,128)(2,1)}, u32[]{:S(2)}, u32[]{:S(2)}) async-start(bf16[8,768,128]{1,2,0:T(8,128)(2,1)} %broadcast_in_dim.19), calls=%async_computation | async-start | bytes 3145728 | tf_op jit(solution)/shard_map/all_to_all | solution.py:107
  54.3 308.1 %all-reduce.2.cloned.1.call-start = ((), (), s32[]{:S(2)}) async-start(), calls=%async_computation.2 | async-start | bytes 11010048 | tf_op jit(solution)/shard_map/psum | solution.py:138
  54.3 96.8 %collective-permute-start.8 = (bf16[896,1280]{1,0:T(8,128)(2,1)}, bf16[896,1280]{1,0:T(8,128)(2,1)}, u32[]{:S(2)}, u32[]{:S(2)}) collective-permute-start(bf16[896,1280]{1,0:T(8,128)(2,1)} %param.22), channel_id=1, source_target_pairs={{0,16},{8,24},{16,0},{24,8},{1,17},{9,25},{17,1},{25,9},{2,18},{10... | collective-permute-start | bytes 6881288 | tf_op jit(solution)/shard_map/ppermute | solution.py:43
  55.8 81.7 %collective-permute-start.4 = (bf16[896,256]{1,0:T(8,128)(2,1)S(1)}, bf16[896,256]{1,0:T(8,128)(2,1)S(1)}, u32[]{:S(2)}, u32[]{:S(2)}) collective-permute-start(bf16[896,256]{1,0:T(8,128)(2,1)S(1)} %copy-done.12), channel_id=1, source_target_pairs={{0,16},{8,24},{16,0},{24,8},{1,17},{9,25},{17,1},{25,9},{2,18},{10... | collective-permute-start | bytes 1376264 | tf_op jit(solution)/shard_map/ppermute | solution.py:43
  138.6 2.8 collective-permute-start.5
  145.9 5.2 %copy-start.9 = (bf16[896,1280]{1,0:T(8,128)(2,1)S(1)}, bf16[896,1280]{1,0:T(8,128)(2,1)}, u32[]{:S(2)}) copy-start(bf16[896,1280]{1,0:T(8,128)(2,1)} %param.22) | copy-start | bytes 6881284
  151.0 26.0 %collective-permute-start.7 = (bf16[2,896,1280]{2,1,0:T(8,128)(2,1)}, bf16[2,896,1280]{2,1,0:T(8,128)(2,1)}, u32[]{:S(2)}, u32[]{:S(2)}) collective-permute-start(bf16[2,896,1280]{2,1,0:T(8,128)(2,1)} %pad_maximum_fusion.3), channel_id=1, source_target_pairs={{0,8},{8,0},{16,24},{24,16},{1,9},{9,1},{17,25},{25,17},{2,10},{10... | collective-permute-start | bytes 13762568 | tf_op jit(solution)/shard_map/ppermute | solution.py:46
  155.2 31.7 %collective-permute-start.9 = (bf16[2,896,1280]{2,1,0:T(8,128)(2,1)}, bf16[2,896,1280]{2,1,0:T(8,128)(2,1)}, u32[]{:S(2)}, u32[]{:S(2)}) collective-permute-start(bf16[2,896,1280]{2,1,0:T(8,128)(2,1)} %pad_maximum_fusion.4), channel_id=1, source_target_pairs={{0,8},{8,0},{16,24},{24,16},{1,9},{9,1},{17,25},{25,17},{2,10},{10... | collective-permute-start | bytes 13762568 | tf_op jit(solution)/shard_map/ppermute | solution.py:46
  170.0 1.8 copy-start.16
  170.0 4.2 copy-start.15
  170.1 4.3 collective-permute-start.12
  171.9 3.5 collective-permute-start
  175.4 1.2 collective-permute-start.1
  177.0 9.9 %copy-start.10 = (bf16[896,1280]{1,0:T(8,128)(2,1)S(1)}, bf16[896,1280]{1,0:T(8,128)(2,1)}, u32[]{:S(2)}) copy-start(bf16[896,1280]{1,0:T(8,128)(2,1)} %param.22) | copy-start | bytes 6881284
  362.4 11.9 %copy-start.2 = (bf16[768,896]{1,0:T(8,128)(2,1)S(1)}, bf16[768,896]{1,0:T(8,128)(2,1)}, u32[]{:S(2)}) copy-start(bf16[768,896]{1,0:T(8,128)(2,1)} %copy-done.1) | copy-start | bytes 4128772
  362.4 11.9 %copy-start.4 = (bf16[768,896]{1,0:T(8,128)(2,1)S(1)}, bf16[768,896]{1,0:T(8,128)(2,1)}, u32[]{:S(2)}) copy-start(bf16[768,896]{1,0:T(8,128)(2,1)} %copy-done.3) | copy-start | bytes 4128772
  362.4 11.9 %copy-start.6 = (bf16[768,896]{1,0:T(8,128)(2,1)S(1)}, bf16[768,896]{1,0:T(8,128)(2,1)}, u32[]{:S(2)}) copy-start(bf16[768,896]{1,0:T(8,128)(2,1)} %copy-done.5) | copy-start | bytes 4128772
  362.4 11.9 %copy-start.8 = (bf16[768,896]{1,0:T(8,128)(2,1)S(1)}, bf16[768,896]{1,0:T(8,128)(2,1)}, u32[]{:S(2)}) copy-start(bf16[768,896]{1,0:T(8,128)(2,1)} %copy-done.7) | copy-start | bytes 4128772
  362.4 11.9 %copy-start.11 = (bf16[4,896,1280]{2,1,0:T(8,128)(2,1)S(1)}, bf16[4,896,1280]{2,1,0:T(8,128)(2,1)}, u32[]{:S(2)}) copy-start(bf16[4,896,1280]{2,1,0:T(8,128)(2,1)} %pad_maximum_fusion.1) | copy-start | bytes 27525124
  400.4 4.5 %collective-permute-start.10 = (f32[16,1280]{1,0:T(8,128)S(1)}, f32[16,1280]{1,0:T(8,128)S(1)}, u32[]{:S(2)}, u32[]{:S(2)}) collective-permute-start(f32[16,1280]{1,0:T(8,128)S(1)} %fusion.9), channel_id=1, source_target_pairs={{0,16},{8,24},{16,0},{24,8},{1,17},{9,25},{17,1},{25,9},{2,18},{10... | collective-permute-start | bytes 245768 | tf_op jit(solution)/shard_map/ppermute | solution.py:43
  404.9 2.6 collective-permute-start.11
  411.7 31.3 %all-to-all-start.1 = ((f32[32,16,448]{2,1,0:T(8,128)}), f32[32,16,448]{2,1,0:T(8,128)S(1)}, u32[]{:S(2)}, u32[]{:S(2)}) async-start(f32[32,16,448]{2,1,0:T(8,128)} %bitcast.103), calls=%async_computation.1 | async-start | bytes 2097152 | tf_op jit(solution)/shard_map/all_to_all | solution.py:195
  415.4 1.2 collective-permute-start.13
Sparse Core Ops, SparseCore 0:
  170.2 192.1 all-reduce.1
where the time goes:
time: 452 us; the launch traced here: 451 us
  waiting for transfers between devices  295 us (65%)
  other arithmetic  55.5 us (12%)
  matrix products  46.4 us (10%)
  starting transfers between devices  20 us (4%)
  between operations  17 us (4%)
  local copies, waits for them, and re-layouts  16.4 us (4%)
    psum x1, waiting for transfers between devices, on_device(): lax.psum(attn_term.astype(jnp.bfloat16), 'tp').astype(jnp.float32)  167 us
    ppermute x7, waiting for transfers between devices, gather_grp(): moving = lax.ppermute(moving, 'grp', ring)  98.4 us
    all_to_all x1, waiting for transfers between devices, on_device(): lax.all_to_all(send.reshape(grp_size * tp_size, slots, d_tp), ('grp', 'tp...  26.1 us
    concatenate x6, other arithmetic, gather_grp(): return jnp.concatenate([mine, other], 0)  23 us
    dot_general x1, matrix products, on_device(): jnp.dot(selector.astype(jnp.bfloat16), hidden_ffn, preferred_element_type...  14.4 us
    another operation x7, other arithmetic, gather_grp(): mine = jnp.stack(held)  13.7 us
    add x1, other arithmetic, on_device(): residual = hidden_perm.astype(jnp.float32) + attn_total  11.9 us
    dot_general x1, matrix products, on_device(): up_pre = jnp.dot(norm_mid, up_full, preferred_element_type=jnp.float32)  11.6 us
  transfers between devices with their start and end apart: 17, of which 9 were waited for; matrix products, arithmetic and copies ran while one was open for 16% of the time, Pallas kernels for 0%

commit v1 on v0

--- a/solution.py
+++ b/solution.py
@@ -135,7 +135,9 @@
     )
     attended_rows = attended_rows.astype(jnp.bfloat16).reshape(row_count, local_heads * HEAD_SIZE)
     attn_term = transposed_dot(attended_rows, o_full)
-    attn_total = lax.psum(attn_term.astype(jnp.bfloat16), "tp").astype(jnp.float32)
+    attn_total = jnp.sum(lax.all_gather(attn_term.astype(jnp.bfloat16), "tp"), axis=0).astype(
+        jnp.float32
+    )
     residual = hidden_perm.astype(jnp.float32) + attn_total
     norm_mid = rms_scale(residual, ffn_gain_perm)
     gate_pre = jnp.dot(norm_mid, gate_full, preferred_element_type=jnp.float32)

time: 452 us -> 1050 us (2.32)
  waiting for transfers between devices: 295 us -> 874 us
  other arithmetic: 55.5 us -> 70.7 us
    all_gather x0 -> x1, waiting for transfers between devices: none -> 705 us  [on_device(): lax.all_gather(attn_term.astype(jnp.bfloat16), 'tp')]
    psum x1 -> x0, waiting for transfers between devices: 167 us -> none  [on_device(): lax.psum(attn_term.astype(jnp.bfloat16), 'tp').astype(jnp.float32)]
    ppermute x7, waiting for transfers between devices: 98.4 us -> 121 us  [gather_grp(): moving = lax.ppermute(moving, 'grp', ring)]
    reduce_sum x0 -> x1, other arithmetic: none -> 18.1 us  [on_device(): jnp.sum(lax.all_gather(attn_term.astype(jnp.bfloat16), 'tp'), axis=0)]
    all_to_all x1, waiting for transfers between devices: 0.01 us -> 16.5 us  [on_device(): lax.all_to_all(jnp.broadcast_to(kv_part[None], (tp_size,) + kv_part.shape...]
  transfers between devices with their start and end apart: 17 -> 17, of which waited for: 9 -> 12; matrix products, arithmetic and copies ran while one was open for 16% -> 4% of each run, Pallas kernels for 0% -> 0%
where the time goes in v1:
time: 1050 us
  waiting for transfers between devices  874 us (83%)
  other arithmetic  70.7 us (7%)
  matrix products  48.3 us (5%)
  starting transfers between devices  21.6 us (2%)
  between operations  17 us (2%)
  local copies, waits for them, and re-layouts  16.2 us (2%)
    all_gather x1, waiting for transfers between devices, on_device(): lax.all_gather(attn_term.astype(jnp.bfloat16), 'tp')  705 us
    ppermute x7, waiting for transfers between devices, gather_grp(): moving = lax.ppermute(moving, 'grp', ring)  121 us
    all_to_all x1, waiting for transfers between devices, on_device(): lax.all_to_all(send.reshape(grp_size * tp_size, slots, d_tp), ('grp', 'tp...  26.1 us
    concatenate x6, other arithmetic, gather_grp(): return jnp.concatenate([mine, other], 0)  22.1 us
  transfers between devices with their start and end apart: 17, of which 12 were waited for; matrix products, arithmetic and copies ran while one was open for 4% of the time, Pallas kernels for 0%

profile of v1, /device:TPU:0, one launch (start us, length us, event | category | flops | bytes accessed | tf_op | source)
XLA Modules:
  0.0 1047.4 jit_solution(4563804473616701375)
XLA Ops:
  6.5 1.2 copy.59
  7.8 1.1 copy.60
  8.8 2.0 pad_maximum_fusion.9
  10.9 2.9 collective-permute-start.2
  15.6 1.2 fusion.76
  16.8 12.8 %collective-permute-done.2 = bf16[896,384]{1,0:T(8,128)(2,1)} collective-permute-done((bf16[896,384]{1,0:T(8,128)(2,1)}, bf16[896,384]{1,0:T(8,128)(2,1)}, u32[]{:S(2)}, u32[]{:S(2)}) %collective-permute-start.2) | collective-permute-done | bytes 688160 | tf_op jit(solution)/shard_map/ppermute | solution.py:43
  29.5 2.3 pad_maximum_fusion.7
  33.9 3.1 constant_dynamic-slice_fusion.5
  37.0 1.4 fusion.1
  38.4 2.3 pad_maximum_fusion.5
  40.7 4.1 fusion.12
  45.8 1.3 broadcast_in_dim.19
  47.1 6.1 all-to-all-start
  53.4 1.5 collective-permute-start.4
  54.9 11.1 %collective-permute-done.4 = bf16[896,256]{1,0:T(8,128)(2,1)S(1)} collective-permute-done((bf16[896,256]{1,0:T(8,128)(2,1)S(1)}, bf16[896,256]{1,0:T(8,128)(2,1)S(1)}, u32[]{:S(2)}, u32[]{:S(2)}) %collective-permute-start.4) | collective-permute-done | bytes 458784 | tf_op jit(solution)/shard_map/ppermute | solution.py:43
  66.1 1.0 pad_maximum_fusion.8
  67.4 0.9 broadcast_compare_fusion
  68.3 1.6 collective-permute-done.5
  69.9 2.6 pad_maximum_fusion.6
  72.5 1.0 slice.47
  74.4 16.5 %all-to-all-done = bf16[8,768,128]{1,2,0:T(8,128)(2,1)} async-done(((bf16[8,768,128]{1,2,0:T(8,128)(2,1)}), bf16[8,768,128]{1,2,0:T(8,128)(2,1)}, u32[]{:S(2)}, u32[]{:S(2)}) %all-to-all-start) | async-done | bytes 1572896 | tf_op jit(solution)/shard_map/all_to_all | solution.py:107
  90.9 1.5 fusion.58
  93.6 3.5 fusion.63
  97.1 2.0 fusion.15
  99.5 5.5 convolution_convert_fusion
  105.1 1.6 collective-permute-start.8
  107.1 51.0 %collective-permute-done.8 = bf16[896,1280]{1,0:T(8,128)(2,1)S(1)} collective-permute-done((bf16[896,1280]{1,0:T(8,128)(2,1)}, bf16[896,1280]{1,0:T(8,128)(2,1)S(1)}, u32[]{:S(2)}, u32[]{:S(2)}) %collective-permute-start.8) | collective-permute-done | bytes 2293792 | tf_op jit(solution)/shard_map/ppermute | solution.py:43
  158.1 5.1 pad_maximum_fusion.4
  163.3 42.4 %collective-permute-done.6 = bf16[896,1280]{1,0:T(8,128)(2,1)S(1)} collective-permute-done((bf16[896,1280]{1,0:T(8,128)(2,1)}, bf16[896,1280]{1,0:T(8,128)(2,1)S(1)}, u32[]{:S(2)}, u32[]{:S(2)}) %collective-permute-start.6) | collective-permute-done | bytes 2293792 | tf_op jit(solution)/shard_map/ppermute | solution.py:43
  205.6 2.8 pad_maximum_fusion.3
  208.5 1.6 collective-permute-start.12
  212.5 1.2 collective-permute-done
  213.8 2.4 collective-permute-done.1
  216.6 10.2 pad_maximum_fusion.1
  226.7 7.0 pad_maximum_fusion
  233.7 704.9 %all-gather.3.cloned.1.call-done = bf16[6144,3584]{1,0:T(8,128)(2,1)} async-done(((bf16[768,3584]{1,0:T(8,128)(2,1)}), bf16[6144,3584]{1,0:T(8,128)(2,1)}) %all-gather.3.cloned.1.call-update) | async-done | bytes 44040208 | tf_op jit(solution)/shard_map/all_gather | solution.py:138
  938.6 18.1 %reduce_sum.74 = bf16[768,3584]{1,0:T(8,128)(2,1)} reduce(bf16[8,768,3584]{2,1,0:T(8,128)(2,1)} %bitcast.97, bf16[]{:T(256)} %constant.113.clone.1), dimensions={0}, to_apply=%region_7.8 | reduce | flops 19267584 | bytes 49545216 | tf_op jit(solution)/shard_map/reduce_sum | solution.py:138
  956.8 11.3 %convert_add_fusion = (f32[768,3584]{1,0:T(8,128)}, f32[768]{0:T(1024)S(1)}) fusion(bf16[768,3584]{1,0:T(8,128)(2,1)} %reduce_sum.74, bf16[768,896]{1,0:T(8,128)(2,1)} %copy-done.6, bf16[768,896]{1,0:T(8,128)(2,1)} %copy-done.8, bf16[768,896]{1,0:T(8,128)(2,1)} %copy-done.4, bf16[768,896]{1,0:T(8,128)(2,1)} %copy-done.2), kind=kLoop, calls=%fused_computation.1 | loop fusion | flops 33029376 | bytes 22023168 | tf_op jit(solution)/shard_map/add | solution.py:141
  968.1 13.6 %fusion.56 = f32[768,1280]{1,0:T(8,128)} fusion(bf16[3584,1280]{1,0:T(8,128)(2,1)} %bitcast.106, f32[3584]{0:T(1024)S(1)} %pad_maximum_fusion.13, f32[768]{0:T(1024)S(1)} %add_rsqrt_fusion, bf16[768,3584]{1,0:T(8,128)(2,1)S(1)} %copy-done.1, bf16[768,896]{1,0:T(8,128)(2,1)S(1)} %copy-done.7, bf16[768,896]{1,0:T(8,128)(2,1)S(1)} %copy-done.9, ...), kind=kOutput, calls=%fused_computation.111 | convolution fusion | flops 7082213376 | bytes 24134656 | tf_op jit(solution)/shard_map/dot_general | solution.py:144
  981.7 14.5 %fusion.9 = f32[16,1280]{1,0:T(8,128)S(1)} fusion(f32[768,1280]{1,0:T(8,128)} %fusion.56, s32[768]{0:T(1024)S(1)} %add.141, bf16[3584,1280]{1,0:T(8,128)(2,1)} %bitcast.107, f32[3584]{0:T(1024)S(1)} %pad_maximum_fusion.13, f32[768]{0:T(1024)S(1)} %add_rsqrt_fusion, bf16[768,3584]{1,0:T(8,128)(2,1)} %reduce_sum.74, bf16[768,896]{1,0:T(8,128)(2,1)} %copy-done.6, ...), kind=kOutput, calls=%fused_computation.24 | convolution fusion | flops 7119605760 | bytes 24219648 | tf_op jit(solution)/shard_map/dot_general | solution.py:150
  996.2 1.5 collective-permute-start.10
  997.9 2.8 collective-permute-done.10
  1000.9 2.3 fusion.21
  1003.3 2.1 convolution_bitcast_fusion.1
  1006.4 1.1 copy.73
  1007.5 4.7 all-to-all-start.1
  1012.5 0.9 collective-permute-done.13
  1013.7 26.1 %all-to-all-done.1 = f32[32,16,448]{2,1,0:T(8,128)S(1)} async-done(((f32[32,16,448]{2,1,0:T(8,128)}), f32[32,16,448]{2,1,0:T(8,128)S(1)}, u32[]{:S(2)}, u32[]{:S(2)}) %all-to-all-start.1) | async-done | bytes 917536 | tf_op jit(solution)/shard_map/all_to_all | solution.py:197
  (116 shorter events, 10.8 us)
Async XLA Ops:
  6.5 996.8 %copy-start = (bf16[896,1280]{1,0:T(8,128)(2,1)S(1)}, bf16[896,1280]{1,0:T(8,128)(2,1)}, u32[]{:S(2)}) copy-start(bf16[896,1280]{1,0:T(8,128)(2,1)} %param.23) | copy-start | bytes 6881284
  6.5 27.2 %copy-start.17 = (f32[3584]{0:T(1024)S(1)}, f32[3584]{0:T(1024)}, u32[]{:S(2)}) copy-start(f32[3584]{0:T(1024)} %param.15) | copy-start | bytes 43012
  10.9 18.7 %collective-permute-start.2 = (bf16[896,384]{1,0:T(8,128)(2,1)}, bf16[896,384]{1,0:T(8,128)(2,1)}, u32[]{:S(2)}, u32[]{:S(2)}) collective-permute-start(bf16[896,384]{1,0:T(8,128)(2,1)} %pad_maximum_fusion.9), channel_id=1, source_target_pairs={{0,16},{8,24},{16,0},{24,8},{1,17},{9,25},{17,1},{25,9},{2,18},{10... | collective-permute-start | bytes 2064392 | tf_op jit(solution)/shard_map/ppermute | solution.py:43
  31.9 6.5 collective-permute-start.3
  36.9 3.7 copy-start.2
  36.9 3.7 copy-start.4
  37.0 3.7 copy-start.6
  37.0 3.7 copy-start.8
  44.8 0.8 copy-start.16
  45.6 7.8 copy-start.15
  45.6 21.5 %copy-start.20 = (s32[2,8]{1,0:T(2,128)S(1)}, s32[2,8]{1,0:T(2,128)}, u32[]{:S(2)}) copy-start(s32[2,8]{1,0:T(2,128)} %param.13) | copy-start | bytes 196
  47.1 43.9 %all-to-all-start = ((bf16[8,768,128]{1,2,0:T(8,128)(2,1)}), bf16[8,768,128]{1,2,0:T(8,128)(2,1)}, u32[]{:S(2)}, u32[]{:S(2)}) async-start(bf16[8,768,128]{1,2,0:T(8,128)(2,1)} %broadcast_in_dim.19), calls=%async_computation | async-start | bytes 3145728 | tf_op jit(solution)/shard_map/all_to_all | solution.py:107
  53.2 885.5 %all-gather.3.cloned.1.call-start = ((), (), s32[]{:S(2)}) async-start(), calls=%async_computation.2 | async-start | bytes 49545216 | tf_op jit(solution)/shard_map/all_gather | solution.py:138
  53.4 12.7 %collective-permute-start.4 = (bf16[896,256]{1,0:T(8,128)(2,1)S(1)}, bf16[896,256]{1,0:T(8,128)(2,1)S(1)}, u32[]{:S(2)}, u32[]{:S(2)}) collective-permute-start(bf16[896,256]{1,0:T(8,128)(2,1)S(1)} %copy-done.15), channel_id=1, source_target_pairs={{0,16},{8,24},{16,0},{24,8},{1,17},{9,25},{17,1},{25,9},{2,18},{10... | collective-permute-start | bytes 1376264 | tf_op jit(solution)/shard_map/ppermute | solution.py:43
  67.1 2.8 collective-permute-start.5
  105.1 53.1 %collective-permute-start.8 = (bf16[896,1280]{1,0:T(8,128)(2,1)}, bf16[896,1280]{1,0:T(8,128)(2,1)S(1)}, u32[]{:S(2)}, u32[]{:S(2)}) collective-permute-start(bf16[896,1280]{1,0:T(8,128)(2,1)} %param.22), channel_id=1, source_target_pairs={{0,16},{8,24},{16,0},{24,8},{1,17},{9,25},{17,1},{25,9},{2,18},{10... | collective-permute-start | bytes 6881288 | tf_op jit(solution)/shard_map/ppermute | solution.py:43
  106.7 99.0 %collective-permute-start.6 = (bf16[896,1280]{1,0:T(8,128)(2,1)}, bf16[896,1280]{1,0:T(8,128)(2,1)S(1)}, u32[]{:S(2)}, u32[]{:S(2)}) collective-permute-start(bf16[896,1280]{1,0:T(8,128)(2,1)} %param.21), channel_id=1, source_target_pairs={{0,16},{8,24},{16,0},{24,8},{1,17},{9,25},{17,1},{25,9},{2,18},{10... | collective-permute-start | bytes 6881288 | tf_op jit(solution)/shard_map/ppermute | solution.py:43
  158.1 5.1 copy-start.14
  158.1 47.5 %copy-start.10 = (bf16[896,1280]{1,0:T(8,128)(2,1)S(1)}, bf16[896,1280]{1,0:T(8,128)(2,1)}, u32[]{:S(2)}) copy-start(bf16[896,1280]{1,0:T(8,128)(2,1)} %param.21) | copy-start | bytes 6881284
  163.2 53.3 %collective-permute-start.9 = (bf16[2,896,1280]{2,1,0:T(8,128)(2,1)}, bf16[2,896,1280]{2,1,0:T(8,128)(2,1)}, u32[]{:S(2)}, u32[]{:S(2)}) collective-permute-start(bf16[2,896,1280]{2,1,0:T(8,128)(2,1)} %pad_maximum_fusion.4), channel_id=1, source_target_pairs={{0,8},{8,0},{16,24},{24,16},{1,9},{9,1},{17,25},{25,17},{2,10},{10... | collective-permute-start | bytes 13762568 | tf_op jit(solution)/shard_map/ppermute | solution.py:46
  205.6 2.8 copy-start.12
  205.6 4.5 copy-start.19
  205.6 6.7 copy-start.18
  208.4 18.3 %collective-permute-start.7 = (bf16[2,896,1280]{2,1,0:T(8,128)(2,1)}, bf16[2,896,1280]{2,1,0:T(8,128)(2,1)}, u32[]{:S(2)}, u32[]{:S(2)}) collective-permute-start(bf16[2,896,1280]{2,1,0:T(8,128)(2,1)} %pad_maximum_fusion.3), channel_id=1, source_target_pairs={{0,8},{8,0},{16,24},{24,16},{1,9},{9,1},{17,25},{25,17},{2,10},{10... | collective-permute-start | bytes 13762568 | tf_op jit(solution)/shard_map/ppermute | solution.py:46
  208.5 3.9 collective-permute-start.12
  210.1 3.5 collective-permute-start
  213.7 2.5 collective-permute-start.1
  216.6 10.2 copy-start.11
  216.6 10.2 copy-start.13
  956.8 11.3 %copy-start.1 = (bf16[768,3584]{1,0:T(8,128)(2,1)S(1)}, bf16[768,3584]{1,0:T(8,128)(2,1)}, u32[]{:S(2)}) copy-start(bf16[768,3584]{1,0:T(8,128)(2,1)} %reduce_sum.74) | copy-start | bytes 16515076
  956.8 11.3 %copy-start.3 = (bf16[768,896]{1,0:T(8,128)(2,1)S(1)}, bf16[768,896]{1,0:T(8,128)(2,1)}, u32[]{:S(2)}) copy-start(bf16[768,896]{1,0:T(8,128)(2,1)} %copy-done.2) | copy-start | bytes 4128772
  956.8 11.3 %copy-start.5 = (bf16[768,896]{1,0:T(8,128)(2,1)S(1)}, bf16[768,896]{1,0:T(8,128)(2,1)}, u32[]{:S(2)}) copy-start(bf16[768,896]{1,0:T(8,128)(2,1)} %copy-done.4) | copy-start | bytes 4128772
  956.8 11.3 %copy-start.7 = (bf16[768,896]{1,0:T(8,128)(2,1)S(1)}, bf16[768,896]{1,0:T(8,128)(2,1)}, u32[]{:S(2)}) copy-start(bf16[768,896]{1,0:T(8,128)(2,1)} %copy-done.6) | copy-start | bytes 4128772
  956.8 11.3 %copy-start.9 = (bf16[768,896]{1,0:T(8,128)(2,1)S(1)}, bf16[768,896]{1,0:T(8,128)(2,1)}, u32[]{:S(2)}) copy-start(bf16[768,896]{1,0:T(8,128)(2,1)} %copy-done.8) | copy-start | bytes 4128772
  996.2 4.5 collective-permute-start.10
  1000.7 2.6 collective-permute-start.11
  1007.5 32.3 %all-to-all-start.1 = ((f32[32,16,448]{2,1,0:T(8,128)}), f32[32,16,448]{2,1,0:T(8,128)S(1)}, u32[]{:S(2)}, u32[]{:S(2)}) async-start(f32[32,16,448]{2,1,0:T(8,128)} %bitcast.109), calls=%async_computation.1 | async-start | bytes 2097152 | tf_op jit(solution)/shard_map/all_to_all | solution.py:197
  1012.2 1.2 collective-permute-start.13
Sparse Core Ops, SparseCore 0:
  105.2 833.4 all-gather.2
